TPU v7x, 256 devices: a whole 4x4x8 slice. The times are simulated.
256 devices in a mesh: row: 4 (over y), col: 16 (over z_hi, x, core), dep: 4 (over z_lo).
Axes of the slice: x: 4, y: 4, z: 8 (z_hi: 2, z_lo: 4; z = z_hi * 4 + z_lo), core: 2. Of those that a mesh axis runs over, the one named last changes fastest.
Arguments:
- grad_out: bfloat16 [4, 512, 12288], P('row', 'dep', 'col'), may hold values from -7 to 7
- out_weight: bfloat16 [8192, 12288], P('row', 'col'), may hold values from -0.09375 to 0.09375
- query_rows: bfloat16 [2048, 8192], P('dep', ('row', 'col')), may hold values from -6 to 6
- key_rows: bfloat16 [2048, 8192], P('dep', ('row', 'col')), may hold values from -6 to 6
- value_rows: bfloat16 [2048, 8192], P('dep', ('row', 'col')), may hold values from -7 to 7
- seg_lengths: int32 [8], replicated, may hold values from 1 to 1536, 2048 in all
Outputs:
- grad_weight: float32 [8192, 12288], P('row', 'col')
- grad_query: bfloat16 [2048, 8192], P('dep', ('row', 'col'))
- grad_key: bfloat16 [2048, 8192], P('dep', ('row', 'col'))
- grad_value: bfloat16 [2048, 8192], P('dep', ('row', 'col'))
All inputs are finite; a program needn't handle non-finite values.
Results may differ from a plain program's by a relative error of at most 0.029.
Values may be sent and summed in bfloat16 or wider, within the bound.
No kernel may reach another device: no remote copies, remote signals or barrier semaphores. Data moves between devices by JAX's collectives and lax.ppermute only.
A program may use at most 128 MiB of HBM per device.

v0:
```python
import math
import jax
import jax.numpy as jnp
from jax import lax
from jax.sharding import Mesh
from jax.sharding import PartitionSpec as P

NEG_FILL = -1e30
FAR = 1 << 30
COL = ("zh", "x", "core")
DEP = "zl"


def segment_count(positions, seg_ends):
    return jnp.sum((positions[:, None] >= seg_ends[None, :]).astype(jnp.int32), axis=1)


def shift(x, axis, n, s):
    return lax.ppermute(x, axis, [(i, (i + s) % n) for i in range(n)])


def shift_open(x, axis, n, s):
    return lax.ppermute(x, axis, [(i, i + s) for i in range(n) if 0 <= i + s < n])


def roll_rows(x, amount, axis):
    size = x.shape[axis]
    doubled = jnp.concatenate([x, x], axis=axis)
    return lax.dynamic_slice_in_dim(doubled, (size - amount) % size, size, axis=axis)


def rolled_gather(x, axis, n, stack_axis=0):
    parts = [x] + [shift(x, axis, n, -s) for s in range(1, n)]
    return jnp.stack(parts, axis=stack_axis)


def pp_reduce_scatter(x, axis, n, dim):
    me = lax.axis_index(axis)
    acc = lax.dynamic_index_in_dim(x, me, dim, keepdims=False).astype(jnp.float32)
    for s in range(1, n):
        send = lax.dynamic_index_in_dim(x, (me + s) % n, dim, keepdims=False)
        acc = acc + shift(send, axis, n, s).astype(jnp.float32)
    return acc


def pp_reduce_scatter_cols(x, axis, n):
    me = lax.axis_index(axis)
    width = x.shape[1] // n
    acc = lax.dynamic_slice_in_dim(x, me * width, width, axis=1).astype(jnp.float32)
    for s in range(1, n):
        send = lax.dynamic_slice_in_dim(x, (me + s) % n * width, width, axis=1)
        acc = acc + shift(send, axis, n, s).astype(jnp.float32)
    return acc


def make_shards(n_zh, n_x, n_core, n_row, n_dep):

    def shards(grad_out, out_weight, query_rows, key_rows, value_rows, seg_lengths):
        n_tok, feat = (grad_out.shape[1], grad_out.shape[2])
        tok_depth = n_row * n_tok
        head_dim = query_rows.shape[1]
        inv_root = 1.0 / math.sqrt(head_dim)
        me_r = lax.axis_index("row")
        me_d = lax.axis_index(DEP)
        local = grad_out[0]
        grad_rows = rolled_gather(local, "row", n_row).reshape(tok_depth, feat)
        kv = jnp.concatenate([key_rows, value_rows], axis=1)
        kv_all = jnp.stack(
            [kv] + [shift_open(kv, DEP, n_dep, t) for t in range(1, n_dep)], axis=0
        ).reshape(n_dep * tok_depth, 2 * head_dim)
        keys_all, values_all = (kv_all[:, :head_dim], kv_all[:, head_dim:])
        by_depth = rolled_gather(local, DEP, n_dep)
        src_depth = me_d - jnp.arange(n_dep, dtype=jnp.int32)
        key_pos = (
            jnp.where(src_depth >= 0, src_depth * tok_depth, FAR)[:, None]
            + jnp.arange(tok_depth, dtype=jnp.int32)[None, :]
        ).reshape(-1)
        seg_ends = jnp.cumsum(seg_lengths)
        key_seg = segment_count(key_pos, seg_ends)
        query_rows = roll_rows(query_rows, -me_r * n_tok, 0)
        query_pos = (
            me_d * tok_depth + (jnp.arange(tok_depth, dtype=jnp.int32) + me_r * n_tok) % tok_depth
        )
        query_seg = segment_count(query_pos, seg_ends)
        allowed = (query_seg[:, None] == key_seg[None, :]) & (
            key_pos[None, :] <= query_pos[:, None]
        )
        scores = (
            jnp.einsum("qh,kh->qk", query_rows, keys_all, preferred_element_type=jnp.float32)
            * inv_root
        )
        masked = jnp.where(allowed, scores, NEG_FILL)
        row_max = jnp.max(masked, axis=1, keepdims=True)
        exponent = jnp.where(allowed, jnp.exp(masked - row_max), 0.0)
        row_sum = jnp.sum(exponent, axis=1, keepdims=True)
        prob_full = exponent * (1.0 / row_sum)
        prob_half = prob_full.astype(jnp.bfloat16)
        context = jnp.dot(prob_half, values_all, preferred_element_type=jnp.float32).astype(
            jnp.bfloat16
        )
        weight_perm = jnp.transpose(
            out_weight.reshape(n_zh, n_x, n_core, head_dim, feat), (2, 1, 0, 3, 4)
        ).reshape(-1, feat)
        partial = jnp.einsum(
            "tf,hf->th", grad_rows, weight_perm, preferred_element_type=jnp.float32
        ).astype(jnp.bfloat16)
        partial = pp_reduce_scatter_cols(partial, "core", n_core).astype(jnp.bfloat16)
        context, partial, by_depth = lax.optimization_barrier((context, partial, by_depth))
        by_depth = roll_rows(by_depth, me_d, 0)
        rows_all = rolled_gather(by_depth, "row", n_row, stack_axis=1)
        ctx_all = lax.all_gather(context[None], ("zh", DEP, "x", "core"), axis=0, tiled=True)
        ctx_all = ctx_all.reshape(n_zh, n_dep, n_x, n_core, tok_depth, head_dim)
        partial = pp_reduce_scatter_cols(partial, "x", n_x).astype(jnp.bfloat16)
        partial = pp_reduce_scatter_cols(partial, "zh", n_zh).astype(jnp.bfloat16)
        context_grad = partial
        grad_prob = jnp.dot(context_grad, values_all.T, preferred_element_type=jnp.float32)
        delta_row = jnp.sum(prob_full * grad_prob, axis=1, keepdims=True)
        grad_score = (prob_full * (grad_prob - delta_row)).astype(jnp.bfloat16)
        grad_query = (
            jnp.dot(grad_score, keys_all, preferred_element_type=jnp.float32) * inv_root
        ).astype(jnp.bfloat16)
        key_partial = (
            jnp.einsum("qk,qh->kh", grad_score, query_rows, preferred_element_type=jnp.float32)
            * inv_root
        ).astype(jnp.bfloat16)
        value_partial = jnp.einsum(
            "qk,qh->kh", prob_half, context_grad, preferred_element_type=jnp.float32
        ).astype(jnp.bfloat16)
        kv_partial = jnp.concatenate([key_partial, value_partial], axis=1).reshape(
            n_dep, tok_depth, 2 * head_dim
        )
        kv_grad = kv_partial[0].astype(jnp.float32)
        for s in range(1, n_dep):
            kv_grad = kv_grad + shift_open(kv_partial[s], DEP, n_dep, -s).astype(jnp.float32)
        kv_grad = kv_grad.astype(jnp.bfloat16)
        grad_key, grad_value = (kv_grad[:, :head_dim], kv_grad[:, head_dim:])
        grad_weight = None
        for depth in range(n_dep):
            piece = jnp.einsum(
                "zxcth,tf->zxchf",
                ctx_all[:, depth],
                rows_all[depth].reshape(tok_depth, feat),
                preferred_element_type=jnp.float32,
            )
            grad_weight = piece if grad_weight is None else grad_weight + piece
            if depth < n_dep - 1:
                grad_weight = lax.optimization_barrier(grad_weight)
        grad_weight = grad_weight.reshape(n_zh * n_x * n_core * head_dim, feat)
        grad_query = roll_rows(grad_query, me_r * n_tok, 0)
        return (grad_weight, grad_query, grad_key, grad_value)

    return shards


def solution(mesh):
    n_row, n_col, n_dep = (mesh.shape["row"], mesh.shape["col"], mesh.shape["dep"])
    n_zh, n_core = (2, 2)
    n_x = n_col // (n_zh * n_core)
    fine = Mesh(mesh.devices.reshape(n_row, n_zh, n_x, n_core, n_dep), ("row",) + COL + (DEP,))
    in_specs = (
        P("row", DEP, COL),
        P("row", COL),
        P(DEP, ("row",) + COL),
        P(DEP, ("row",) + COL),
        P(DEP, ("row",) + COL),
        P(),
    )
    out_specs = (
        P("row", COL),
        P(DEP, ("row",) + COL),
        P(DEP, ("row",) + COL),
        P(DEP, ("row",) + COL),
    )
    return jax.shard_map(
        make_shards(n_zh, n_x, n_core, n_row, n_dep),
        mesh=fine,
        in_specs=in_specs,
        out_specs=out_specs,
        check_vma=False,
    )
```

profile of v0, /device:TPU:1, one launch (start us, length us, event | category | flops | bytes accessed | tf_op | source)
XLA Modules:
  0.0 173.1 jit_solution(16478914064638914497)
XLA Ops:
  7.2 2.5 %collective-permute-start.9 = (bf16[128,768]{1,0:T(8,128)(2,1)}, bf16[128,768]{1,0:T(8,128)(2,1)S(1)}, u32[]{:S(2)}, u32[]{:S(2)}) collective-permute-start(bf16[128,768]{1,0:T(8,128)(2,1)} %bitcast.94), channel_id=1, source_target_pairs={{0,1},{1,2},{2,3},{3,0},{4,5},{5,6},{6,7},{7,4},{8,9},{9,10},{10,1... | collective-permute-start | bytes 589832 | tf_op jit(solution)/shard_map/ppermute | solution.py:19
  9.8 3.0 %collective-permute-start.8 = (bf16[128,768]{1,0:T(8,128)(2,1)}, bf16[128,768]{1,0:T(8,128)(2,1)S(1)}, u32[]{:S(2)}, u32[]{:S(2)}) collective-permute-start(bf16[128,768]{1,0:T(8,128)(2,1)} %bitcast.95), channel_id=1, source_target_pairs={{0,2},{1,3},{2,0},{3,1},{4,6},{5,7},{6,4},{7,5},{8,10},{9,11},{10,... | collective-permute-start | bytes 589832 | tf_op jit(solution)/shard_map/ppermute | solution.py:19
  12.8 0.7 collective-permute-start.7
  13.5 1.3 collective-permute-start.5
  14.8 2.6 %collective-permute-start.4 = (bf16[128,768]{1,0:T(8,128)(2,1)}, bf16[128,768]{1,0:T(8,128)(2,1)S(1)}, u32[]{:S(2)}, u32[]{:S(2)}) collective-permute-start(bf16[128,768]{1,0:T(8,128)(2,1)} %bitcast.98), channel_id=1, source_target_pairs={{0,128},{64,192},{128,0},{192,64},{1,129},{65,193},{129,1},{193,65... | collective-permute-start | bytes 589832 | tf_op jit(solution)/shard_map/ppermute | solution.py:19
  17.4 0.8 reduce-window.8
  18.3 3.8 %copy.29 = bf16[2,4,2,128,768]{4,3,2,1,0:T(8,128)(2,1)} copy(bf16[2,4,2,128,768]{4,3,0,1,2:T(8,128)(2,1)} %bitcast.86) | data formatting | bytes 6291456 | tf_op jit(solution)/shard_map/transpose | solution.py:101
  22.3 1.1 collective-permute-start.3
  23.6 2.9 %collective-permute-done.8 = bf16[128,768]{1,0:T(8,128)(2,1)S(1)} collective-permute-done((bf16[128,768]{1,0:T(8,128)(2,1)}, bf16[128,768]{1,0:T(8,128)(2,1)S(1)}, u32[]{:S(2)}, u32[]{:S(2)}) %collective-permute-start.8) | collective-permute-done | bytes 196640 | tf_op jit(solution)/shard_map/ppermute | solution.py:19
  26.5 6.1 %collective-permute-start.2 = (bf16[512,256]{1,0:T(8,128)(2,1)S(1)}, bf16[512,256]{1,0:T(8,128)(2,1)S(1)}, u32[]{:S(2)}, u32[]{:S(2)}) collective-permute-start(bf16[512,256]{1,0:T(8,128)(2,1)S(1)} %constant_dynamic-update-slice_fusion), channel_id=1, source_target_pairs={{0,3},{4,7},{8,11},{12,15},{16,19},{20,23},{24,27},{28,31},{32,35}... | collective-permute-start | bytes 786440 | tf_op jit(solution)/shard_map/ppermute | solution.py:23
  32.6 1.3 collective-permute-start.1
  33.9 2.2 %collective-permute-start = (bf16[512,256]{1,0:T(8,128)(2,1)S(1)}, bf16[512,256]{1,0:T(8,128)(2,1)S(1)}, u32[]{:S(2)}, u32[]{:S(2)}) collective-permute-start(bf16[512,256]{1,0:T(8,128)(2,1)S(1)} %constant_dynamic-update-slice_fusion), channel_id=1, source_target_pairs={{0,1},{1,2},{2,3},{4,5},{5,6},{6,7},{8,9},{9,10},{10,11},{12,13},{... | collective-permute-start | bytes 786440 | tf_op jit(solution)/shard_map/ppermute | solution.py:23
  36.3 3.7 %convolution_convert_fusion = bf16[512,2048]{1,0:T(8,128)(2,1)S(1)} fusion(bf16[512,768]{1,0:T(8,128)(2,1)S(1)} %bitcast.89, bf16[2048,768]{1,0:T(8,128)(2,1)} %bitcast.87), kind=kOutput, calls=%fused_computation.8 | convolution fusion | flops 1611661312 | bytes 6029312 | tf_op jit(solution)/shard_map/tf,hf->th/dot_general | solution.py:104
  40.2 2.2 %collective-permute-start.6 = (bf16[512,1024]{1,0:T(8,128)(2,1)S(1)}, bf16[512,1024]{1,0:T(8,128)(2,1)}, u32[]{:S(2)}, u32[]{:S(2)}) collective-permute-start(bf16[512,1024]{1,0:T(8,128)(2,1)S(1)} %constant_dynamic-slice_fusion.4), channel_id=1, source_target_pairs={{0,4},{4,0},{1,5},{5,1},{2,6},{6,2},{3,7},{7,3},{8,12},{12,8},{9,1... | collective-permute-start | bytes 3145736 | tf_op jit(solution)/shard_map/ppermute | solution.py:19
  42.4 5.6 %collective-permute-done = bf16[512,256]{1,0:T(8,128)(2,1)S(1)} collective-permute-done((bf16[512,256]{1,0:T(8,128)(2,1)S(1)}, bf16[512,256]{1,0:T(8,128)(2,1)S(1)}, u32[]{:S(2)}, u32[]{:S(2)}) %collective-permute-start) | collective-permute-done | bytes 262176 | tf_op jit(solution)/shard_map/ppermute | solution.py:23
  48.1 1.6 fusion
  49.7 1.7 fusion.26
  51.4 2.0 %copy-done = f32[512,2048]{1,0:T(8,128)} copy-done((f32[512,2048]{1,0:T(8,128)}, f32[512,2048]{1,0:T(8,128)S(1)}, u32[]{:S(2)}) %copy-start) | copy-done | bytes 4194328
  53.4 1.4 convolution_convert_fusion.2
  54.8 1.9 %add_convert_fusion = bf16[512,1024]{1,0:T(8,128)(2,1)S(1)} fusion(bf16[512,1024]{1,0:T(8,128)(2,1)} %collective-permute-done.6, bf16[512,2048]{1,0:T(8,128)(2,1)} %copy-done.3, s32[]{:T(128)S(6)} %select_n.99), kind=kLoop, calls=%fused_computation.20 | loop fusion | flops 2097152 | bytes 3145732 | tf_op jit(solution)/shard_map/convert_element_type | solution.py:107
  56.9 1.0 constant_dynamic-slice_fusion.3
  57.8 1.2 collective-permute-start.13
  59.0 1.5 collective-permute-start.15
  60.5 1.5 collective-permute-start.14
  62.0 2.4 %collective-permute-done.13 = bf16[512,256]{1,0:T(8,128)(2,1)S(1)} collective-permute-done((bf16[512,256]{1,0:T(8,128)(2,1)}, bf16[512,256]{1,0:T(8,128)(2,1)S(1)}, u32[]{:S(2)}, u32[]{:S(2)}) %collective-permute-start.13) | collective-permute-done | bytes 262176 | tf_op jit(solution)/shard_map/ppermute | solution.py:19
  64.7 6.3 %collective-permute-done.14 = bf16[512,256]{1,0:T(8,128)(2,1)} collective-permute-done((bf16[512,256]{1,0:T(8,128)(2,1)S(1)}, bf16[512,256]{1,0:T(8,128)(2,1)}, u32[]{:S(2)}, u32[]{:S(2)}) %collective-permute-start.14) | collective-permute-done | bytes 262176 | tf_op jit(solution)/shard_map/ppermute | solution.py:19
  71.0 1.2 add_convert_fusion.2
  72.2 5.2 %collective-permute-start.16 = (bf16[512,128]{1,0:T(8,128)(2,1)S(1)}, bf16[512,128]{1,0:T(8,128)(2,1)S(1)}, u32[]{:S(2)}, u32[]{:S(2)}) collective-permute-start(bf16[512,128]{1,0:T(8,128)(2,1)S(1)} %constant_dynamic-slice_fusion), channel_id=1, source_target_pairs={{0,32},{32,0},{1,33},{33,1},{2,34},{34,2},{3,35},{35,3},{4,36},{36... | collective-permute-start | bytes 393224 | tf_op jit(solution)/shard_map/ppermute | solution.py:19
  77.4 2.6 %collective-permute-done.16 = bf16[512,128]{1,0:T(8,128)(2,1)S(1)} collective-permute-done((bf16[512,128]{1,0:T(8,128)(2,1)S(1)}, bf16[512,128]{1,0:T(8,128)(2,1)S(1)}, u32[]{:S(2)}, u32[]{:S(2)}) %collective-permute-start.16) | collective-permute-done | bytes 131104 | tf_op jit(solution)/shard_map/ppermute | solution.py:19
  80.0 3.0 %multiply_reduce_fusion = (f32[512]{0:T(512)S(1)}, f32[512,2048]{1,0:T(8,128)S(1)}) fusion(f32[512,2048]{1,0:T(8,128)} %copy-done, f32[512]{0:T(512)S(1)} %broadcast_divide_fusion, bf16[2048,256]{1,0:T(8,128)(2,1)S(1)} %bitcast.80, bf16[512,128]{1,0:T(8,128)(2,1)S(1)} %collective-permute-done.16, bf16[512,256]{1,0:T(8,128)(2,1)S(1)} %add_convert_fusion.2, ...), kind=kOutput, calls=%fused_computation.1 | convolution fusion | flops 271842816 | bytes 9179140 | tf_op jit(solution)/shard_map/dot_general | solution.py:116
  83.6 0.9 fusion.1
  85.2 1.3 collective-permute-start.17
  86.5 1.2 fusion.8
  87.7 2.7 %collective-permute-start.10 = (bf16[4,128,768]{2,1,0:T(8,128)(2,1)}, bf16[4,128,768]{2,1,0:T(8,128)(2,1)S(1)}, u32[]{:S(2)}, u32[]{:S(2)}) collective-permute-start(bf16[4,128,768]{2,1,0:T(8,128)(2,1)} %fusion.8), channel_id=1, source_target_pairs={{0,192},{64,0},{128,64},{192,128},{1,193},{65,1},{129,65},{193,129... | collective-permute-start | bytes 2359304 | tf_op jit(solution)/shard_map/ppermute | solution.py:19
  91.7 1.3 collective-permute-start.19
  93.0 13.5 %collective-permute-done.17 = bf16[512,256]{0,1:T(8,128)(2,1)S(1)} collective-permute-done((bf16[512,256]{0,1:T(8,128)(2,1)S(1)}, bf16[512,256]{0,1:T(8,128)(2,1)S(1)}, u32[]{:S(2)}, u32[]{:S(2)}) %collective-permute-start.17) | collective-permute-done | bytes 262176 | tf_op jit(solution)/shard_map/ppermute | solution.py:23
  106.5 1.5 collective-permute-start.18
  108.7 1.2 fusion.18
  109.9 3.1 %collective-permute-done.19 = bf16[512,256]{0,1:T(8,128)(2,1)S(1)} collective-permute-done((bf16[512,256]{0,1:T(8,128)(2,1)S(1)}, bf16[512,256]{0,1:T(8,128)(2,1)S(1)}, u32[]{:S(2)}, u32[]{:S(2)}) %collective-permute-start.19) | collective-permute-done | bytes 262176 | tf_op jit(solution)/shard_map/ppermute | solution.py:23
  113.0 19.4 %collective-permute-done.18 = bf16[512,256]{0,1:T(8,128)(2,1)S(1)} collective-permute-done((bf16[512,256]{0,1:T(8,128)(2,1)S(1)}, bf16[512,256]{0,1:T(8,128)(2,1)S(1)}, u32[]{:S(2)}, u32[]{:S(2)}) %collective-permute-start.18) | collective-permute-done | bytes 262176 | tf_op jit(solution)/shard_map/ppermute | solution.py:23
  132.6 0.8 copy.35
  133.3 0.8 copy.34
  134.1 1.6 pad_maximum_fusion
  136.0 18.1 %all-gather.3.cloned.1.call-done = bf16[32768,128]{1,0:T(8,128)(2,1)} async-done(((bf16[512,128]{1,0:T(8,128)(2,1)}), bf16[32768,128]{1,0:T(8,128)(2,1)}) %all-gather.3.cloned.1.call-update) | async-done | bytes 8388624 | tf_op jit(solution)/shard_map/all_gather | solution.py:111
  154.1 3.6 %fusion.2 = f32[2,4,2,128,768]{4,3,2,1,0:T(8,128)S(1)} fusion(bf16[512,768,1,1,1]{1,0,4,3,2:T(8,128)(2,1)S(1)} %bitcast.85, bf16[2,4,4,2,512,128]{5,4,3,2,1,0:T(8,128)(2,1)} %bitcast.73), kind=kOutput, calls=%fused_computation.19 | convolution fusion | flops 1610612736 | bytes 9175040 | tf_op jit(solution)/shard_map/zxcth,tf->zxchf/dot_general | solution.py:139
  158.1 1.8 %convolution_add_fusion.2 = f32[2,4,2,128,768]{4,3,2,1,0:T(8,128)S(1)} fusion(f32[2,4,2,128,768]{4,3,2,1,0:T(8,128)S(1)} %fusion.2, bf16[512,768,1,1,1]{1,0,4,3,2:T(8,128)(2,1)S(1)} %bitcast.84, bf16[2,4,4,2,512,128]{5,4,3,2,1,0:T(8,128)(2,1)S(1)} %bitcast.74), kind=kOutput, calls=%fused_computation.11 | convolution fusion | flops 1612185600 | bytes 15466496 | tf_op jit(solution)/shard_map/zxcth,tf->zxchf/dot_general | solution.py:139
  159.9 1.8 %convolution_add_fusion.1 = f32[2,4,2,128,768]{4,3,2,1,0:T(8,128)S(1)} fusion(f32[2,4,2,128,768]{4,3,2,1,0:T(8,128)S(1)} %convolution_add_fusion.2, bf16[512,768,1,1,1]{1,0,4,3,2:T(8,128)(2,1)S(1)} %bitcast.83, bf16[2,4,4,2,512,128]{5,4,3,2,1,0:T(8,128)(2,1)S(1)} %bitcast.75), kind=kOutput, calls=%fused_computation.10 | convolution fusion | flops 1612185600 | bytes 15466496 | tf_op jit(solution)/shard_map/zxcth,tf->zxchf/dot_general | solution.py:139
  161.7 4.5 %convolution_add_fusion = f32[2,4,2,128,768]{4,3,2,1,0:T(8,128)} fusion(f32[2,4,2,128,768]{4,3,2,1,0:T(8,128)S(1)} %convolution_add_fusion.1, bf16[512,768,1,1,1]{1,0,4,3,2:T(8,128)(2,1)S(1)} %bitcast.82, bf16[2,4,4,2,512,128]{5,4,3,2,1,0:T(8,128)(2,1)S(1)} %bitcast.76), kind=kOutput, calls=%fused_computation.9 | convolution fusion | flops 1612185600 | bytes 15466496 | tf_op jit(solution)/shard_map/zxcth,tf->zxchf/dot_general | solution.py:139
  (52 shorter events, 5.2 us)
Async XLA Ops:
  7.2 15.2 %copy-start.4 = (bf16[1,128,768]{2,1,0:T(8,128)(2,1)S(1)}, bf16[1,128,768]{2,1,0:T(8,128)(2,1)}, u32[]{:S(2)}) copy-start(bf16[1,128,768]{2,1,0:T(8,128)(2,1)} %param.6) | copy-start | bytes 589828
  7.2 15.1 %copy-start.5 = (bf16[512,128]{1,0:T(8,128)(2,1)S(1)}, bf16[512,128]{1,0:T(8,128)(2,1)}, u32[]{:S(2)}) copy-start(bf16[512,128]{1,0:T(8,128)(2,1)} %param.9) | copy-start | bytes 393220
  7.2 16.4 %copy-start.6 = (bf16[512,128]{1,0:T(8,128)(2,1)S(1)}, bf16[512,128]{1,0:T(8,128)(2,1)}, u32[]{:S(2)}) copy-start(bf16[512,128]{1,0:T(8,128)(2,1)} %param.10) | copy-start | bytes 393220
  7.2 146.9 %all-gather.3.cloned.1.call-start = ((), (), s32[]{:S(2)}) async-start(), calls=%async_computation | async-start | bytes 8519680 | tf_op jit(solution)/shard_map/all_gather | solution.py:111
  7.2 15.1 %collective-permute-start.9 = (bf16[128,768]{1,0:T(8,128)(2,1)}, bf16[128,768]{1,0:T(8,128)(2,1)S(1)}, u32[]{:S(2)}, u32[]{:S(2)}) collective-permute-start(bf16[128,768]{1,0:T(8,128)(2,1)} %bitcast.94), channel_id=1, source_target_pairs={{0,1},{1,2},{2,3},{3,0},{4,5},{5,6},{6,7},{7,4},{8,9},{9,10},{10,1... | collective-permute-start | bytes 589832 | tf_op jit(solution)/shard_map/ppermute | solution.py:19
  9.8 16.7 %collective-permute-start.8 = (bf16[128,768]{1,0:T(8,128)(2,1)}, bf16[128,768]{1,0:T(8,128)(2,1)S(1)}, u32[]{:S(2)}, u32[]{:S(2)}) collective-permute-start(bf16[128,768]{1,0:T(8,128)(2,1)} %bitcast.95), channel_id=1, source_target_pairs={{0,2},{1,3},{2,0},{3,1},{4,6},{5,7},{6,4},{7,5},{8,10},{9,11},{10,... | collective-permute-start | bytes 589832 | tf_op jit(solution)/shard_map/ppermute | solution.py:19
  12.8 19.8 %collective-permute-start.7 = (bf16[128,768]{1,0:T(8,128)(2,1)}, bf16[128,768]{1,0:T(8,128)(2,1)S(1)}, u32[]{:S(2)}, u32[]{:S(2)}) collective-permute-start(bf16[128,768]{1,0:T(8,128)(2,1)} %bitcast.96), channel_id=1, source_target_pairs={{0,3},{1,0},{2,1},{3,2},{4,7},{5,4},{6,5},{7,6},{8,11},{9,8},{10,9... | collective-permute-start | bytes 589832 | tf_op jit(solution)/shard_map/ppermute | solution.py:19
  13.5 20.4 %collective-permute-start.5 = (bf16[128,768]{1,0:T(8,128)(2,1)}, bf16[128,768]{1,0:T(8,128)(2,1)S(1)}, u32[]{:S(2)}, u32[]{:S(2)}) collective-permute-start(bf16[128,768]{1,0:T(8,128)(2,1)} %bitcast.97), channel_id=1, source_target_pairs={{0,64},{64,128},{128,192},{192,0},{1,65},{65,129},{129,193},{193,1... | collective-permute-start | bytes 589832 | tf_op jit(solution)/shard_map/ppermute | solution.py:19
  14.8 21.3 %collective-permute-start.4 = (bf16[128,768]{1,0:T(8,128)(2,1)}, bf16[128,768]{1,0:T(8,128)(2,1)S(1)}, u32[]{:S(2)}, u32[]{:S(2)}) collective-permute-start(bf16[128,768]{1,0:T(8,128)(2,1)} %bitcast.98), channel_id=1, source_target_pairs={{0,128},{64,192},{128,0},{192,64},{1,129},{65,193},{129,1},{193,65... | collective-permute-start | bytes 589832 | tf_op jit(solution)/shard_map/ppermute | solution.py:19
  22.3 13.8 %collective-permute-start.3 = (bf16[128,768]{1,0:T(8,128)(2,1)S(1)}, bf16[128,768]{1,0:T(8,128)(2,1)S(1)}, u32[]{:S(2)}, u32[]{:S(2)}) collective-permute-start(bf16[128,768]{1,0:T(8,128)(2,1)S(1)} %bitcast.99), channel_id=1, source_target_pairs={{0,192},{64,0},{128,64},{192,128},{1,193},{65,1},{129,65},{193,129... | collective-permute-start | bytes 589832 | tf_op jit(solution)/shard_map/ppermute | solution.py:19
  26.5 15.9 %collective-permute-start.2 = (bf16[512,256]{1,0:T(8,128)(2,1)S(1)}, bf16[512,256]{1,0:T(8,128)(2,1)S(1)}, u32[]{:S(2)}, u32[]{:S(2)}) collective-permute-start(bf16[512,256]{1,0:T(8,128)(2,1)S(1)} %constant_dynamic-update-slice_fusion), channel_id=1, source_target_pairs={{0,3},{4,7},{8,11},{12,15},{16,19},{20,23},{24,27},{28,31},{32,35}... | collective-permute-start | bytes 786440 | tf_op jit(solution)/shard_map/ppermute | solution.py:23
  32.6 9.8 %collective-permute-start.1 = (bf16[512,256]{1,0:T(8,128)(2,1)S(1)}, bf16[512,256]{1,0:T(8,128)(2,1)S(1)}, u32[]{:S(2)}, u32[]{:S(2)}) collective-permute-start(bf16[512,256]{1,0:T(8,128)(2,1)S(1)} %constant_dynamic-update-slice_fusion), channel_id=1, source_target_pairs={{0,2},{1,3},{4,6},{5,7},{8,10},{9,11},{12,14},{13,15},{16,18},{17,... | collective-permute-start | bytes 786440 | tf_op jit(solution)/shard_map/ppermute | solution.py:23
  33.9 14.0 %collective-permute-start = (bf16[512,256]{1,0:T(8,128)(2,1)S(1)}, bf16[512,256]{1,0:T(8,128)(2,1)S(1)}, u32[]{:S(2)}, u32[]{:S(2)}) collective-permute-start(bf16[512,256]{1,0:T(8,128)(2,1)S(1)} %constant_dynamic-update-slice_fusion), channel_id=1, source_target_pairs={{0,1},{1,2},{2,3},{4,5},{5,6},{6,7},{8,9},{9,10},{10,11},{12,13},{... | collective-permute-start | bytes 786440 | tf_op jit(solution)/shard_map/ppermute | solution.py:23
  40.0 8.0 %copy-start.3 = (bf16[512,2048]{1,0:T(8,128)(2,1)}, bf16[512,2048]{1,0:T(8,128)(2,1)S(1)}, u32[]{:S(2)}) copy-start(bf16[512,2048]{1,0:T(8,128)(2,1)S(1)} %convolution_convert_fusion) | copy-start | bytes 6291460
  40.0 8.0 %copy-start.7 = (bf16[512,128]{1,0:T(8,128)(2,1)S(1)}, bf16[512,128]{1,0:T(8,128)(2,1)}, u32[]{:S(2)}) copy-start(bf16[512,128]{1,0:T(8,128)(2,1)} %param.8) | copy-start | bytes 393220
  40.2 14.7 %collective-permute-start.6 = (bf16[512,1024]{1,0:T(8,128)(2,1)S(1)}, bf16[512,1024]{1,0:T(8,128)(2,1)}, u32[]{:S(2)}, u32[]{:S(2)}) collective-permute-start(bf16[512,1024]{1,0:T(8,128)(2,1)S(1)} %constant_dynamic-slice_fusion.4), channel_id=1, source_target_pairs={{0,4},{4,0},{1,5},{5,1},{2,6},{6,2},{3,7},{7,3},{8,12},{12,8},{9,1... | collective-permute-start | bytes 3145736 | tf_op jit(solution)/shard_map/ppermute | solution.py:19
  51.4 2.0 %copy-start = (f32[512,2048]{1,0:T(8,128)}, f32[512,2048]{1,0:T(8,128)S(1)}, u32[]{:S(2)}) copy-start(f32[512,2048]{1,0:T(8,128)S(1)} %get-tuple-element.27) | copy-start | bytes 12582916
  57.8 6.6 %collective-permute-start.13 = (bf16[512,256]{1,0:T(8,128)(2,1)}, bf16[512,256]{1,0:T(8,128)(2,1)S(1)}, u32[]{:S(2)}, u32[]{:S(2)}) collective-permute-start(bf16[512,256]{1,0:T(8,128)(2,1)} %get-tuple-element.35), channel_id=1, source_target_pairs={{0,8},{8,16},{16,24},{24,0},{1,9},{9,17},{17,25},{25,1},{2,10},{10... | collective-permute-start | bytes 786440 | tf_op jit(solution)/shard_map/ppermute | solution.py:19
  59.0 5.6 %collective-permute-start.15 = (bf16[512,256]{1,0:T(8,128)(2,1)}, bf16[512,256]{1,0:T(8,128)(2,1)}, u32[]{:S(2)}, u32[]{:S(2)}) collective-permute-start(bf16[512,256]{1,0:T(8,128)(2,1)} %get-tuple-element.36), channel_id=1, source_target_pairs={{0,24},{8,0},{16,8},{24,16},{1,25},{9,1},{17,9},{25,17},{2,26},{10... | collective-permute-start | bytes 786440 | tf_op jit(solution)/shard_map/ppermute | solution.py:19
  60.5 10.5 %collective-permute-start.14 = (bf16[512,256]{1,0:T(8,128)(2,1)S(1)}, bf16[512,256]{1,0:T(8,128)(2,1)}, u32[]{:S(2)}, u32[]{:S(2)}) collective-permute-start(bf16[512,256]{1,0:T(8,128)(2,1)S(1)} %get-tuple-element.37), channel_id=1, source_target_pairs={{0,16},{8,24},{16,0},{24,8},{1,17},{9,25},{17,1},{25,9},{2,18},{10... | collective-permute-start | bytes 786440 | tf_op jit(solution)/shard_map/ppermute | solution.py:19
  72.2 7.8 %collective-permute-start.16 = (bf16[512,128]{1,0:T(8,128)(2,1)S(1)}, bf16[512,128]{1,0:T(8,128)(2,1)S(1)}, u32[]{:S(2)}, u32[]{:S(2)}) collective-permute-start(bf16[512,128]{1,0:T(8,128)(2,1)S(1)} %constant_dynamic-slice_fusion), channel_id=1, source_target_pairs={{0,32},{32,0},{1,33},{33,1},{2,34},{34,2},{3,35},{35,3},{4,36},{36... | collective-permute-start | bytes 393224 | tf_op jit(solution)/shard_map/ppermute | solution.py:19
  77.4 5.6 %copy-start.1 = (f32[512,2048]{1,0:T(8,128)S(1)}, f32[512,2048]{1,0:T(8,128)}, u32[]{:S(2)}) copy-start(f32[512,2048]{1,0:T(8,128)} %copy-done) | copy-start | bytes 12582916
  85.2 21.3 %collective-permute-start.17 = (bf16[512,256]{0,1:T(8,128)(2,1)S(1)}, bf16[512,256]{0,1:T(8,128)(2,1)S(1)}, u32[]{:S(2)}, u32[]{:S(2)}) collective-permute-start(bf16[512,256]{0,1:T(8,128)(2,1)S(1)} %get-tuple-element.32), channel_id=1, source_target_pairs={{1,0},{2,1},{3,2},{5,4},{6,5},{7,6},{9,8},{10,9},{11,10},{13,12},{... | collective-permute-start | bytes 786440 | tf_op jit(solution)/shard_map/ppermute | solution.py:23
  87.7 46.4 %collective-permute-start.10 = (bf16[4,128,768]{2,1,0:T(8,128)(2,1)}, bf16[4,128,768]{2,1,0:T(8,128)(2,1)S(1)}, u32[]{:S(2)}, u32[]{:S(2)}) collective-permute-start(bf16[4,128,768]{2,1,0:T(8,128)(2,1)} %fusion.8), channel_id=1, source_target_pairs={{0,192},{64,0},{128,64},{192,128},{1,193},{65,1},{129,65},{193,129... | collective-permute-start | bytes 2359304 | tf_op jit(solution)/shard_map/ppermute | solution.py:19
  90.4 43.7 %collective-permute-start.11 = (bf16[4,128,768]{2,1,0:T(8,128)(2,1)}, bf16[4,128,768]{2,1,0:T(8,128)(2,1)}, u32[]{:S(2)}, u32[]{:S(2)}) collective-permute-start(bf16[4,128,768]{2,1,0:T(8,128)(2,1)} %fusion.8), channel_id=1, source_target_pairs={{0,128},{64,192},{128,0},{192,64},{1,129},{65,193},{129,1},{193,65... | collective-permute-start | bytes 2359304 | tf_op jit(solution)/shard_map/ppermute | solution.py:19
  90.8 43.3 %collective-permute-start.12 = (bf16[4,128,768]{2,1,0:T(8,128)(2,1)}, bf16[4,128,768]{2,1,0:T(8,128)(2,1)}, u32[]{:S(2)}, u32[]{:S(2)}) collective-permute-start(bf16[4,128,768]{2,1,0:T(8,128)(2,1)} %fusion.8), channel_id=1, source_target_pairs={{0,64},{64,128},{128,192},{192,0},{1,65},{65,129},{129,193},{193,1... | collective-permute-start | bytes 2359304 | tf_op jit(solution)/shard_map/ppermute | solution.py:19
  91.7 21.3 %collective-permute-start.19 = (bf16[512,256]{0,1:T(8,128)(2,1)S(1)}, bf16[512,256]{0,1:T(8,128)(2,1)S(1)}, u32[]{:S(2)}, u32[]{:S(2)}) collective-permute-start(bf16[512,256]{0,1:T(8,128)(2,1)S(1)} %get-tuple-element.33), channel_id=1, source_target_pairs={{3,0},{7,4},{11,8},{15,12},{19,16},{23,20},{27,24},{31,28},{35,32}... | collective-permute-start | bytes 786440 | tf_op jit(solution)/shard_map/ppermute | solution.py:23
  106.5 25.9 %collective-permute-start.18 = (bf16[512,256]{0,1:T(8,128)(2,1)S(1)}, bf16[512,256]{0,1:T(8,128)(2,1)S(1)}, u32[]{:S(2)}, u32[]{:S(2)}) collective-permute-start(bf16[512,256]{0,1:T(8,128)(2,1)S(1)} %get-tuple-element.34), channel_id=1, source_target_pairs={{2,0},{3,1},{6,4},{7,5},{10,8},{11,9},{14,12},{15,13},{18,16},{19,... | collective-permute-start | bytes 786440 | tf_op jit(solution)/shard_map/ppermute | solution.py:23
  154.0 4.0 %copy-start.2 = (bf16[32768,128]{1,0:T(8,128)(2,1)S(1)}, bf16[32768,128]{1,0:T(8,128)(2,1)}, u32[]{:S(2)}) copy-start(bf16[32768,128]{1,0:T(8,128)(2,1)} %all-gather.3.cloned.1.call-done) | copy-start | bytes 25165828
Sparse Core Ops, SparseCore 0:
  56.9 97.0 all-gather.2
where the time goes:
time: 174 us; the launch traced here: 173 us
  waiting for transfers between devices  74.1 us (43%)
  starting transfers between devices  40.4 us (23%)
  matrix products  23.8 us (14%)
  between operations  14.4 us (8%)
  other arithmetic  11.2 us (6%)
  local copies, waits for them, and re-layouts  9.22 us (5%)
    ppermute x6, waiting for transfers between devices, shift_open(): lax.ppermute(x, axis, [(i, i + s) for i in range(n) if 0 <= i + s < n])  41.5 us
    ppermute x14, starting transfers between devices, shift(): return lax.ppermute(x, axis, [(i, (i + s) % n) for i in range(n)])  26.7 us
    all_gather x1, waiting for transfers between devices, shards(): lax.all_gather(context[None], ('zh', DEP, 'x', 'core'), axis=0, tiled=True)  18.1 us
    ppermute x14, waiting for transfers between devices, shift(): return lax.ppermute(x, axis, [(i, (i + s) % n) for i in range(n)])  14.5 us
    ppermute x6, starting transfers between devices, shift_open(): lax.ppermute(x, axis, [(i, i + s) for i in range(n) if 0 <= i + s < n])  13.7 us
    dot_general x4, matrix products, shards(): jnp.einsum('zxcth,tf->zxchf', ctx_all[:, depth], rows_all[depth].reshape(...  11.8 us
    unnamed x20, local copies, waits for them, and re-layouts  4.01 us
    transpose x1, local copies, waits for them, and re-layouts, shards(): jnp.transpose(out_weight.reshape(n_zh, n_x, n_core, head_dim, feat), (2,...  3.83 us
  transfers between devices with their start and end apart: 21, of which 10 were waited for; matrix products, arithmetic and copies ran while one was open for 16% of the time, Pallas kernels for 0%

commit v1 on v0

--- a/solution.py
+++ b/solution.py
@@ -108,7 +108,15 @@
         context, partial, by_depth = lax.optimization_barrier((context, partial, by_depth))
         by_depth = roll_rows(by_depth, me_d, 0)
         rows_all = rolled_gather(by_depth, "row", n_row, stack_axis=1)
-        ctx_all = lax.all_gather(context[None], ("zh", DEP, "x", "core"), axis=0, tiled=True)
+        ctx_all = jnp.concatenate(
+            lax.all_to_all(
+                jnp.stack([context[None]] * lax.axis_size(("zh", DEP, "x", "core"))),
+                ("zh", DEP, "x", "core"),
+                0,
+                0,
+            ),
+            axis=0,
+        )
         ctx_all = ctx_all.reshape(n_zh, n_dep, n_x, n_core, tok_depth, head_dim)
         partial = pp_reduce_scatter_cols(partial, "x", n_x).astype(jnp.bfloat16)
         partial = pp_reduce_scatter_cols(partial, "zh", n_zh).astype(jnp.bfloat16)

time: 174 us -> 331 us (1.90); the launches traced: 173 us -> 326 us
  waiting for transfers between devices: 74.1 us -> 209 us
  starting transfers between devices: 40.4 us -> 64.8 us
  between operations: 14.4 us -> 1.05 us
  local copies, waits for them, and re-layouts: 9.22 us -> 14 us
  matrix products: 23.8 us -> 27.7 us
    ppermute x14, waiting for transfers between devices: 14.5 us -> 182 us  [shift(): return lax.ppermute(x, axis, [(i, (i + s) % n) for i in range(n)])]
    all_to_all x0 -> x1, starting transfers between devices: none -> 19.1 us  [shards(): lax.all_to_all(jnp.stack([context[None]] * lax.axis_size(('zh', DEP, 'x',...]
    all_gather x1 -> x0, waiting for transfers between devices: 18.1 us -> none  [shards(): lax.all_gather(context[None], ('zh', DEP, 'x', 'core'), axis=0, tiled=True)]
    ppermute x6, waiting for transfers between devices: 41.5 us -> 26.5 us  [shift_open(): lax.ppermute(x, axis, [(i, i + s) for i in range(n) if 0 <= i + s < n])]
    ppermute x14, starting transfers between devices: 26.7 us -> 32 us  [shift(): return lax.ppermute(x, axis, [(i, (i + s) % n) for i in range(n)])]
    another operation x0 -> x1, local copies, waits for them, and re-layouts: none -> 5.27 us  [shards(): jnp.stack([context[None]] * lax.axis_size(('zh', DEP, 'x', 'core')))]
    dot_general x4, matrix products: 11.8 us -> 16.4 us  [shards(): jnp.einsum('zxcth,tf->zxchf', ctx_all[:, depth], rows_all[depth].reshape(...]
  transfers between devices with their start and end apart: 21 -> 21, of which waited for: 10 -> 10; matrix products, arithmetic and copies ran while one was open for 16% -> 8% of each run, Pallas kernels for 0% -> 0%
where the time goes in v1:
time: 331 us; the launch traced here: 326 us
  waiting for transfers between devices  209 us (63%)
  starting transfers between devices  64.8 us (20%)
  matrix products  27.7 us (8%)
  local copies, waits for them, and re-layouts  14 us (4%)
  other arithmetic  9.67 us (3%)
    ppermute x14, waiting for transfers between devices, shift(): return lax.ppermute(x, axis, [(i, (i + s) % n) for i in range(n)])  182 us
    ppermute x14, starting transfers between devices, shift(): return lax.ppermute(x, axis, [(i, (i + s) % n) for i in range(n)])  32 us
    ppermute x6, waiting for transfers between devices, shift_open(): lax.ppermute(x, axis, [(i, i + s) for i in range(n) if 0 <= i + s < n])  26.5 us
    all_to_all x1, starting transfers between devices, shards(): lax.all_to_all(jnp.stack([context[None]] * lax.axis_size(('zh', DEP, 'x',...  19.1 us
    dot_general x4, matrix products, shards(): jnp.einsum('zxcth,tf->zxchf', ctx_all[:, depth], rows_all[depth].reshape(...  16.4 us
    ppermute x6, starting transfers between devices, shift_open(): lax.ppermute(x, axis, [(i, i + s) for i in range(n) if 0 <= i + s < n])  13.7 us
  transfers between devices with their start and end apart: 21, of which 10 were waited for; matrix products, arithmetic and copies ran while one was open for 8% of the time, Pallas kernels for 0%

profile of v1, /device:TPU:1, one launch (start us, length us, event | category | flops | bytes accessed | tf_op | source)
XLA Modules:
  0.0 326.1 jit_solution(8723976086212398895)
XLA Ops:
  0.7 2.5 collective-permute-start.9
  3.2 3.0 collective-permute-start.8
  6.9 1.3 collective-permute-start.5
  8.2 2.6 collective-permute-start.4
  10.8 0.8 reduce-window.8
  11.8 3.8 %copy.32 = bf16[2,4,2,128,768]{4,3,2,1,0:T(8,128)(2,1)} copy(bf16[2,4,2,128,768]{4,3,0,1,2:T(8,128)(2,1)} %bitcast.82) | data formatting | bytes 6291456 | tf_op jit(solution)/shard_map/transpose | solution.py:101
  15.8 1.1 collective-permute-start.3
  17.0 2.9 collective-permute-done.8
  19.9 6.1 %collective-permute-start.2 = (bf16[512,256]{1,0:T(8,128)(2,1)S(1)}, bf16[512,256]{1,0:T(8,128)(2,1)S(1)}, u32[]{:S(2)}, u32[]{:S(2)}) collective-permute-start(bf16[512,256]{1,0:T(8,128)(2,1)S(1)} %constant_dynamic-update-slice_fusion), channel_id=1, source_target_pairs={{0,3},{4,7},{8,11},{12,15},{16,19},{20,23},{24,27},{28,31},{32,35}... | collective-permute-start | bytes 786440 | tf_op jit(solution)/shard_map/ppermute | solution.py:23
  26.0 1.3 collective-permute-start.1
  27.3 2.2 collective-permute-start
  29.7 3.7 %convolution_convert_fusion = bf16[512,2048]{1,0:T(8,128)(2,1)S(1)} fusion(bf16[512,768]{1,0:T(8,128)(2,1)S(1)} %bitcast.85, bf16[2048,768]{1,0:T(8,128)(2,1)} %bitcast.83), kind=kOutput, calls=%fused_computation.8 | convolution fusion | flops 1611661312 | bytes 6029312 | tf_op jit(solution)/shard_map/tf,hf->th/dot_general | solution.py:104
  33.6 2.2 collective-permute-start.6
  35.8 5.6 %collective-permute-done = bf16[512,256]{1,0:T(8,128)(2,1)S(1)} collective-permute-done((bf16[512,256]{1,0:T(8,128)(2,1)S(1)}, bf16[512,256]{1,0:T(8,128)(2,1)S(1)}, u32[]{:S(2)}, u32[]{:S(2)}) %collective-permute-start) | collective-permute-done | bytes 262176 | tf_op jit(solution)/shard_map/ppermute | solution.py:23
  41.5 1.6 fusion
  43.1 1.7 fusion.26
  44.8 2.0 copy-done
  48.0 5.3 %stack.70 = bf16[64,1,512,128]{3,2,1,0:T(8,128)(2,1)} broadcast(bf16[512,128]{1,0:T(8,128)(2,1)S(1)} %convolution_convert_fusion.2), dimensions={2,3} | broadcast | bytes 8519680 | tf_op jit(solution)/shard_map/stack | solution.py:113
  53.3 19.1 %all-to-all-start = ((bf16[64,1,512,128]{3,2,1,0:T(8,128)(2,1)}), bf16[64,1,512,128]{3,2,1,0:T(8,128)(2,1)}, u32[]{:S(2)}, u32[]{:S(2)}) async-start(bf16[64,1,512,128]{3,2,1,0:T(8,128)(2,1)} %stack.70), calls=%async_computation | async-start | bytes 16777216 | tf_op jit(solution)/shard_map/all_to_all | solution.py:112
  72.4 0.9 constant_dynamic-slice_fusion.3
  73.4 1.4 collective-permute-start.13
  74.8 1.3 collective-permute-start.15
  76.0 1.7 collective-permute-start.14
  77.7 27.3 %collective-permute-done.13 = bf16[512,256]{1,0:T(8,128)(2,1)S(1)} collective-permute-done((bf16[512,256]{1,0:T(8,128)(2,1)}, bf16[512,256]{1,0:T(8,128)(2,1)S(1)}, u32[]{:S(2)}, u32[]{:S(2)}) %collective-permute-start.13) | collective-permute-done | bytes 262176 | tf_op jit(solution)/shard_map/ppermute | solution.py:19
  105.0 3.8 %collective-permute-done.15 = bf16[512,256]{1,0:T(8,128)(2,1)} collective-permute-done((bf16[512,256]{1,0:T(8,128)(2,1)}, bf16[512,256]{1,0:T(8,128)(2,1)}, u32[]{:S(2)}, u32[]{:S(2)}) %collective-permute-start.15) | collective-permute-done | bytes 262176 | tf_op jit(solution)/shard_map/ppermute | solution.py:19
  108.9 6.3 %collective-permute-done.14 = bf16[512,256]{1,0:T(8,128)(2,1)} collective-permute-done((bf16[512,256]{1,0:T(8,128)(2,1)S(1)}, bf16[512,256]{1,0:T(8,128)(2,1)}, u32[]{:S(2)}, u32[]{:S(2)}) %collective-permute-start.14) | collective-permute-done | bytes 262176 | tf_op jit(solution)/shard_map/ppermute | solution.py:19
  115.1 1.2 add_convert_fusion.2
  116.3 10.3 %collective-permute-start.16 = (bf16[512,128]{1,0:T(8,128)(2,1)S(1)}, bf16[512,128]{1,0:T(8,128)(2,1)S(1)}, u32[]{:S(2)}, u32[]{:S(2)}) collective-permute-start(bf16[512,128]{1,0:T(8,128)(2,1)S(1)} %constant_dynamic-slice_fusion), channel_id=1, source_target_pairs={{0,32},{32,0},{1,33},{33,1},{2,34},{34,2},{3,35},{35,3},{4,36},{36... | collective-permute-start | bytes 393224 | tf_op jit(solution)/shard_map/ppermute | solution.py:19
  126.7 132.6 %collective-permute-done.16 = bf16[512,128]{1,0:T(8,128)(2,1)S(1)} collective-permute-done((bf16[512,128]{1,0:T(8,128)(2,1)S(1)}, bf16[512,128]{1,0:T(8,128)(2,1)S(1)}, u32[]{:S(2)}, u32[]{:S(2)}) %collective-permute-start.16) | collective-permute-done | bytes 131104 | tf_op jit(solution)/shard_map/ppermute | solution.py:19
  259.2 3.0 multiply_reduce_fusion
  262.8 0.9 fusion.1
  264.4 1.3 collective-permute-start.17
  265.7 1.2 fusion.8
  266.9 2.7 collective-permute-start.10
  271.0 1.3 collective-permute-start.19
  272.3 5.5 %collective-permute-done.17 = bf16[512,256]{0,1:T(8,128)(2,1)S(1)} collective-permute-done((bf16[512,256]{0,1:T(8,128)(2,1)S(1)}, bf16[512,256]{0,1:T(8,128)(2,1)S(1)}, u32[]{:S(2)}, u32[]{:S(2)}) %collective-permute-start.17) | collective-permute-done | bytes 262176 | tf_op jit(solution)/shard_map/ppermute | solution.py:23
  277.8 1.5 collective-permute-start.18
  280.0 1.2 fusion.18
  281.2 1.8 collective-permute-done.19
  283.0 13.6 %collective-permute-done.18 = bf16[512,256]{0,1:T(8,128)(2,1)S(1)} collective-permute-done((bf16[512,256]{0,1:T(8,128)(2,1)S(1)}, bf16[512,256]{0,1:T(8,128)(2,1)S(1)}, u32[]{:S(2)}, u32[]{:S(2)}) %collective-permute-start.18) | collective-permute-done | bytes 262176 | tf_op jit(solution)/shard_map/ppermute | solution.py:23
  296.8 0.8 copy.38
  297.6 0.8 copy.37
  298.3 9.5 %collective-permute-done.12 = bf16[4,128,768]{2,1,0:T(8,128)(2,1)} collective-permute-done((bf16[4,128,768]{2,1,0:T(8,128)(2,1)}, bf16[4,128,768]{2,1,0:T(8,128)(2,1)}, u32[]{:S(2)}, u32[]{:S(2)}) %collective-permute-start.12) | collective-permute-done | bytes 786464 | tf_op jit(solution)/shard_map/ppermute | solution.py:19
  307.8 1.6 pad_maximum_fusion
  309.6 3.4 %fusion.2 = f32[2,4,2,128,768]{4,3,2,1,0:T(8,128)S(1)} fusion(bf16[512,768,1,1,1]{1,0,4,3,2:T(8,128)(2,1)S(1)} %bitcast.81, bf16[2,4,4,2,512,128]{5,4,3,2,1,0:T(8,128)(2,1)} %bitcast.18), kind=kOutput, calls=%fused_computation.19 | convolution fusion | flops 1610612736 | bytes 9175040 | tf_op jit(solution)/shard_map/zxcth,tf->zxchf/dot_general | solution.py:147
  313.1 3.4 %convolution_add_fusion.2 = f32[2,4,2,128,768]{4,3,2,1,0:T(8,128)S(1)} fusion(f32[2,4,2,128,768]{4,3,2,1,0:T(8,128)S(1)} %fusion.2, bf16[512,768,1,1,1]{1,0,4,3,2:T(8,128)(2,1)S(1)} %bitcast.80, bf16[2,4,4,2,512,128]{5,4,3,2,1,0:T(8,128)(2,1)} %bitcast.18), kind=kOutput, calls=%fused_computation.11 | convolution fusion | flops 1612185600 | bytes 15466496 | tf_op jit(solution)/shard_map/zxcth,tf->zxchf/dot_general | solution.py:147
  316.5 3.4 %convolution_add_fusion.1 = f32[2,4,2,128,768]{4,3,2,1,0:T(8,128)S(1)} fusion(f32[2,4,2,128,768]{4,3,2,1,0:T(8,128)S(1)} %convolution_add_fusion.2, bf16[512,768,1,1,1]{1,0,4,3,2:T(8,128)(2,1)S(1)} %bitcast.79, bf16[2,4,4,2,512,128]{5,4,3,2,1,0:T(8,128)(2,1)} %bitcast.18), kind=kOutput, calls=%fused_computation.10 | convolution fusion | flops 1612185600 | bytes 15466496 | tf_op jit(solution)/shard_map/zxcth,tf->zxchf/dot_general | solution.py:147
  319.9 6.1 %convolution_add_fusion = f32[2,4,2,128,768]{4,3,2,1,0:T(8,128)} fusion(f32[2,4,2,128,768]{4,3,2,1,0:T(8,128)S(1)} %convolution_add_fusion.1, bf16[512,768,1,1,1]{1,0,4,3,2:T(8,128)(2,1)S(1)} %bitcast.78, bf16[2,4,4,2,512,128]{5,4,3,2,1,0:T(8,128)(2,1)} %bitcast.18), kind=kOutput, calls=%fused_computation.9 | convolution fusion | flops 1612185600 | bytes 15466496 | tf_op jit(solution)/shard_map/zxcth,tf->zxchf/dot_general | solution.py:147
  (48 shorter events, 6.4 us)
Async XLA Ops:
  0.6 15.1 %copy-start.2 = (bf16[1,128,768]{2,1,0:T(8,128)(2,1)S(1)}, bf16[1,128,768]{2,1,0:T(8,128)(2,1)}, u32[]{:S(2)}) copy-start(bf16[1,128,768]{2,1,0:T(8,128)(2,1)} %param.6) | copy-start | bytes 589828
  0.6 15.1 %copy-start.3 = (bf16[512,128]{1,0:T(8,128)(2,1)S(1)}, bf16[512,128]{1,0:T(8,128)(2,1)}, u32[]{:S(2)}) copy-start(bf16[512,128]{1,0:T(8,128)(2,1)} %param.9) | copy-start | bytes 393220
  0.7 16.3 %copy-start.4 = (bf16[512,128]{1,0:T(8,128)(2,1)S(1)}, bf16[512,128]{1,0:T(8,128)(2,1)}, u32[]{:S(2)}) copy-start(bf16[512,128]{1,0:T(8,128)(2,1)} %param.10) | copy-start | bytes 393220
  0.7 15.1 %collective-permute-start.9 = (bf16[128,768]{1,0:T(8,128)(2,1)}, bf16[128,768]{1,0:T(8,128)(2,1)S(1)}, u32[]{:S(2)}, u32[]{:S(2)}) collective-permute-start(bf16[128,768]{1,0:T(8,128)(2,1)} %bitcast.90), channel_id=1, source_target_pairs={{0,1},{1,2},{2,3},{3,0},{4,5},{5,6},{6,7},{7,4},{8,9},{9,10},{10,1... | collective-permute-start | bytes 589832 | tf_op jit(solution)/shard_map/ppermute | solution.py:19
  3.2 16.7 %collective-permute-start.8 = (bf16[128,768]{1,0:T(8,128)(2,1)}, bf16[128,768]{1,0:T(8,128)(2,1)S(1)}, u32[]{:S(2)}, u32[]{:S(2)}) collective-permute-start(bf16[128,768]{1,0:T(8,128)(2,1)} %bitcast.91), channel_id=1, source_target_pairs={{0,2},{1,3},{2,0},{3,1},{4,6},{5,7},{6,4},{7,5},{8,10},{9,11},{10,... | collective-permute-start | bytes 589832 | tf_op jit(solution)/shard_map/ppermute | solution.py:19
  6.2 19.8 %collective-permute-start.7 = (bf16[128,768]{1,0:T(8,128)(2,1)}, bf16[128,768]{1,0:T(8,128)(2,1)S(1)}, u32[]{:S(2)}, u32[]{:S(2)}) collective-permute-start(bf16[128,768]{1,0:T(8,128)(2,1)} %bitcast.92), channel_id=1, source_target_pairs={{0,3},{1,0},{2,1},{3,2},{4,7},{5,4},{6,5},{7,6},{8,11},{9,8},{10,9... | collective-permute-start | bytes 589832 | tf_op jit(solution)/shard_map/ppermute | solution.py:19
  6.9 20.4 %collective-permute-start.5 = (bf16[128,768]{1,0:T(8,128)(2,1)}, bf16[128,768]{1,0:T(8,128)(2,1)S(1)}, u32[]{:S(2)}, u32[]{:S(2)}) collective-permute-start(bf16[128,768]{1,0:T(8,128)(2,1)} %bitcast.93), channel_id=1, source_target_pairs={{0,64},{64,128},{128,192},{192,0},{1,65},{65,129},{129,193},{193,1... | collective-permute-start | bytes 589832 | tf_op jit(solution)/shard_map/ppermute | solution.py:19
  8.2 21.3 %collective-permute-start.4 = (bf16[128,768]{1,0:T(8,128)(2,1)}, bf16[128,768]{1,0:T(8,128)(2,1)S(1)}, u32[]{:S(2)}, u32[]{:S(2)}) collective-permute-start(bf16[128,768]{1,0:T(8,128)(2,1)} %bitcast.94), channel_id=1, source_target_pairs={{0,128},{64,192},{128,0},{192,64},{1,129},{65,193},{129,1},{193,65... | collective-permute-start | bytes 589832 | tf_op jit(solution)/shard_map/ppermute | solution.py:19
  15.8 13.8 %collective-permute-start.3 = (bf16[128,768]{1,0:T(8,128)(2,1)S(1)}, bf16[128,768]{1,0:T(8,128)(2,1)S(1)}, u32[]{:S(2)}, u32[]{:S(2)}) collective-permute-start(bf16[128,768]{1,0:T(8,128)(2,1)S(1)} %bitcast.95), channel_id=1, source_target_pairs={{0,192},{64,0},{128,64},{192,128},{1,193},{65,1},{129,65},{193,129... | collective-permute-start | bytes 589832 | tf_op jit(solution)/shard_map/ppermute | solution.py:19
  19.9 15.9 %collective-permute-start.2 = (bf16[512,256]{1,0:T(8,128)(2,1)S(1)}, bf16[512,256]{1,0:T(8,128)(2,1)S(1)}, u32[]{:S(2)}, u32[]{:S(2)}) collective-permute-start(bf16[512,256]{1,0:T(8,128)(2,1)S(1)} %constant_dynamic-update-slice_fusion), channel_id=1, source_target_pairs={{0,3},{4,7},{8,11},{12,15},{16,19},{20,23},{24,27},{28,31},{32,35}... | collective-permute-start | bytes 786440 | tf_op jit(solution)/shard_map/ppermute | solution.py:23
  26.0 9.8 %collective-permute-start.1 = (bf16[512,256]{1,0:T(8,128)(2,1)S(1)}, bf16[512,256]{1,0:T(8,128)(2,1)S(1)}, u32[]{:S(2)}, u32[]{:S(2)}) collective-permute-start(bf16[512,256]{1,0:T(8,128)(2,1)S(1)} %constant_dynamic-update-slice_fusion), channel_id=1, source_target_pairs={{0,2},{1,3},{4,6},{5,7},{8,10},{9,11},{12,14},{13,15},{16,18},{17,... | collective-permute-start | bytes 786440 | tf_op jit(solution)/shard_map/ppermute | solution.py:23
  27.3 14.0 %collective-permute-start = (bf16[512,256]{1,0:T(8,128)(2,1)S(1)}, bf16[512,256]{1,0:T(8,128)(2,1)S(1)}, u32[]{:S(2)}, u32[]{:S(2)}) collective-permute-start(bf16[512,256]{1,0:T(8,128)(2,1)S(1)} %constant_dynamic-update-slice_fusion), channel_id=1, source_target_pairs={{0,1},{1,2},{2,3},{4,5},{5,6},{6,7},{8,9},{9,10},{10,11},{12,13},{... | collective-permute-start | bytes 786440 | tf_op jit(solution)/shard_map/ppermute | solution.py:23
  33.5 8.0 %copy-start.5 = (bf16[512,128]{1,0:T(8,128)(2,1)S(1)}, bf16[512,128]{1,0:T(8,128)(2,1)}, u32[]{:S(2)}) copy-start(bf16[512,128]{1,0:T(8,128)(2,1)} %param.8) | copy-start | bytes 393220
  33.6 14.0 %collective-permute-start.6 = (bf16[512,1024]{1,0:T(8,128)(2,1)S(1)}, bf16[512,1024]{1,0:T(8,128)(2,1)S(1)}, u32[]{:S(2)}, u32[]{:S(2)}) collective-permute-start(bf16[512,1024]{1,0:T(8,128)(2,1)S(1)} %constant_dynamic-slice_fusion.4), channel_id=1, source_target_pairs={{0,4},{4,0},{1,5},{5,1},{2,6},{6,2},{3,7},{7,3},{8,12},{12,8},{9,1... | collective-permute-start | bytes 3145736 | tf_op jit(solution)/shard_map/ppermute | solution.py:19
  44.8 2.0 copy-start
  53.3 256.3 %all-to-all-start = ((bf16[64,1,512,128]{3,2,1,0:T(8,128)(2,1)}), bf16[64,1,512,128]{3,2,1,0:T(8,128)(2,1)}, u32[]{:S(2)}, u32[]{:S(2)}) async-start(bf16[64,1,512,128]{3,2,1,0:T(8,128)(2,1)} %stack.70), calls=%async_computation | async-start | bytes 16777216 | tf_op jit(solution)/shard_map/all_to_all | solution.py:112
  73.4 31.7 %collective-permute-start.13 = (bf16[512,256]{1,0:T(8,128)(2,1)}, bf16[512,256]{1,0:T(8,128)(2,1)S(1)}, u32[]{:S(2)}, u32[]{:S(2)}) collective-permute-start(bf16[512,256]{1,0:T(8,128)(2,1)} %get-tuple-element.39), channel_id=1, source_target_pairs={{0,8},{8,16},{16,24},{24,0},{1,9},{9,17},{17,25},{25,1},{2,10},{10... | collective-permute-start | bytes 786440 | tf_op jit(solution)/shard_map/ppermute | solution.py:19
  74.8 34.1 %collective-permute-start.15 = (bf16[512,256]{1,0:T(8,128)(2,1)}, bf16[512,256]{1,0:T(8,128)(2,1)}, u32[]{:S(2)}, u32[]{:S(2)}) collective-permute-start(bf16[512,256]{1,0:T(8,128)(2,1)} %get-tuple-element.40), channel_id=1, source_target_pairs={{0,24},{8,0},{16,8},{24,16},{1,25},{9,1},{17,9},{25,17},{2,26},{10... | collective-permute-start | bytes 786440 | tf_op jit(solution)/shard_map/ppermute | solution.py:19
  76.0 39.1 %collective-permute-start.14 = (bf16[512,256]{1,0:T(8,128)(2,1)S(1)}, bf16[512,256]{1,0:T(8,128)(2,1)}, u32[]{:S(2)}, u32[]{:S(2)}) collective-permute-start(bf16[512,256]{1,0:T(8,128)(2,1)S(1)} %get-tuple-element.41), channel_id=1, source_target_pairs={{0,16},{8,24},{16,0},{24,8},{1,17},{9,25},{17,1},{25,9},{2,18},{10... | collective-permute-start | bytes 786440 | tf_op jit(solution)/shard_map/ppermute | solution.py:19
  116.3 142.9 %collective-permute-start.16 = (bf16[512,128]{1,0:T(8,128)(2,1)S(1)}, bf16[512,128]{1,0:T(8,128)(2,1)S(1)}, u32[]{:S(2)}, u32[]{:S(2)}) collective-permute-start(bf16[512,128]{1,0:T(8,128)(2,1)S(1)} %constant_dynamic-slice_fusion), channel_id=1, source_target_pairs={{0,32},{32,0},{1,33},{33,1},{2,34},{34,2},{3,35},{35,3},{4,36},{36... | collective-permute-start | bytes 393224 | tf_op jit(solution)/shard_map/ppermute | solution.py:19
  126.7 135.6 %copy-start.1 = (f32[512,2048]{1,0:T(8,128)S(1)}, f32[512,2048]{1,0:T(8,128)}, u32[]{:S(2)}) copy-start(f32[512,2048]{1,0:T(8,128)} %copy-done) | copy-start | bytes 12582916
  264.4 13.4 %collective-permute-start.17 = (bf16[512,256]{0,1:T(8,128)(2,1)S(1)}, bf16[512,256]{0,1:T(8,128)(2,1)S(1)}, u32[]{:S(2)}, u32[]{:S(2)}) collective-permute-start(bf16[512,256]{0,1:T(8,128)(2,1)S(1)} %get-tuple-element.36), channel_id=1, source_target_pairs={{1,0},{2,1},{3,2},{5,4},{6,5},{7,6},{9,8},{10,9},{11,10},{13,12},{... | collective-permute-start | bytes 786440 | tf_op jit(solution)/shard_map/ppermute | solution.py:23
  266.9 31.4 %collective-permute-start.10 = (bf16[4,128,768]{2,1,0:T(8,128)(2,1)}, bf16[4,128,768]{2,1,0:T(8,128)(2,1)S(1)}, u32[]{:S(2)}, u32[]{:S(2)}) collective-permute-start(bf16[4,128,768]{2,1,0:T(8,128)(2,1)} %fusion.8), channel_id=1, source_target_pairs={{0,192},{64,0},{128,64},{192,128},{1,193},{65,1},{129,65},{193,129... | collective-permute-start | bytes 2359304 | tf_op jit(solution)/shard_map/ppermute | solution.py:19
  269.7 28.7 %collective-permute-start.11 = (bf16[4,128,768]{2,1,0:T(8,128)(2,1)}, bf16[4,128,768]{2,1,0:T(8,128)(2,1)}, u32[]{:S(2)}, u32[]{:S(2)}) collective-permute-start(bf16[4,128,768]{2,1,0:T(8,128)(2,1)} %fusion.8), channel_id=1, source_target_pairs={{0,128},{64,192},{128,0},{192,64},{1,129},{65,193},{129,1},{193,65... | collective-permute-start | bytes 2359304 | tf_op jit(solution)/shard_map/ppermute | solution.py:19
  270.0 37.8 %collective-permute-start.12 = (bf16[4,128,768]{2,1,0:T(8,128)(2,1)}, bf16[4,128,768]{2,1,0:T(8,128)(2,1)}, u32[]{:S(2)}, u32[]{:S(2)}) collective-permute-start(bf16[4,128,768]{2,1,0:T(8,128)(2,1)} %fusion.8), channel_id=1, source_target_pairs={{0,64},{64,128},{128,192},{192,0},{1,65},{65,129},{129,193},{193,1... | collective-permute-start | bytes 2359304 | tf_op jit(solution)/shard_map/ppermute | solution.py:19
  271.0 12.0 %collective-permute-start.19 = (bf16[512,256]{0,1:T(8,128)(2,1)S(1)}, bf16[512,256]{0,1:T(8,128)(2,1)S(1)}, u32[]{:S(2)}, u32[]{:S(2)}) collective-permute-start(bf16[512,256]{0,1:T(8,128)(2,1)S(1)} %get-tuple-element.37), channel_id=1, source_target_pairs={{3,0},{7,4},{11,8},{15,12},{19,16},{23,20},{27,24},{31,28},{35,32}... | collective-permute-start | bytes 786440 | tf_op jit(solution)/shard_map/ppermute | solution.py:23
  277.8 18.8 %collective-permute-start.18 = (bf16[512,256]{0,1:T(8,128)(2,1)S(1)}, bf16[512,256]{0,1:T(8,128)(2,1)S(1)}, u32[]{:S(2)}, u32[]{:S(2)}) collective-permute-start(bf16[512,256]{0,1:T(8,128)(2,1)S(1)} %get-tuple-element.38), channel_id=1, source_target_pairs={{2,0},{3,1},{6,4},{7,5},{10,8},{11,9},{14,12},{15,13},{18,16},{19,... | collective-permute-start | bytes 786440 | tf_op jit(solution)/shard_map/ppermute | solution.py:23
